TPU v7x, 128 devices: a whole 4x4x4 slice. The times are simulated.
128 devices in a mesh: wide: 32 (over x, y, core), narrow: 4 (over z).
Axes of the slice: x: 4, y: 4, z: 4, core: 2. Of those that a mesh axis runs over, the one named last changes fastest.
Arguments:
- raw_samples: bfloat16 [1024, 32, 16384], P(('wide', 'narrow')), as said below
- filter_taps: float32 [64], replicated, may hold values from -0.75 to 0.75
- tile_pairs: int32 [16, 2], replicated, may hold values from 0 to 127, as said below
- tile_owners: int32 [16], replicated, may hold values from 0 to 3, as said below
Outputs:
- correlation_stacks: float32 [32, 64, 512], P('narrow', 'wide')
Inputs may be any that keep to these rules, and one draw needn't show every extreme that they name: `raw_samples`: noise samples, scaled per channel and per window. `tile_pairs`: each row is (source block, receiver block), and the two blocks differ. `tile_owners`: each owner has at most 8 tiles, and some owner has exactly 8.
All inputs are finite; a program needn't handle non-finite values.
Results may differ from a plain program's by a relative error of at most 0.0074.
Values may be sent and summed in bfloat16 or wider, within the bound.
No kernel may reach another device: no remote copies, remote signals or barrier semaphores. Data moves between devices by JAX's collectives and lax.ppermute only.
A program may use at most 128 MiB of HBM per device.

v0:
```python
import math
import jax
import jax.numpy as jnp
from jax import lax
from jax.sharding import PartitionSpec as P

NFFT = 4096
DECIM = 4
NBINS = 1024
SMOOTH = 63
LAGS = 512
BLK = 8
SLOTS = 8
water_level = 0.2
epsilon = 1e-06


def fir_tables(filter_taps, block_size):
    in_rows = jnp.arange(DECIM * block_size, dtype=jnp.int32)[:, None]
    out_cols = jnp.arange(block_size, dtype=jnp.int32)[None, :]
    this_index = DECIM * out_cols + DECIM - 1 - in_rows
    last_index = this_index + DECIM * block_size
    tap_count = filter_taps.shape[0]

    def taps_at(tap_index):
        inside = (tap_index >= 0) & (tap_index < tap_count)
        values = jnp.take(filter_taps, jnp.clip(tap_index, 0, tap_count - 1))
        return jnp.where(inside, values, jnp.zeros_like(values)).astype(jnp.bfloat16)

    return (taps_at(this_index), taps_at(last_index))


def decimate(samples, filter_taps):
    row_count, row_length = samples.shape
    block_size = min(128, row_length // DECIM)
    this_table, last_table = fir_tables(filter_taps, block_size)
    segments = samples.reshape(-1, DECIM * block_size)
    current = jnp.dot(segments, this_table, preferred_element_type=jnp.float32).reshape(
        row_count, -1, block_size
    )
    spilled = jnp.dot(segments, last_table, preferred_element_type=jnp.float32).reshape(
        row_count, -1, block_size
    )
    spilled = jnp.pad(spilled[:, :-1], ((0, 0), (1, 0), (0, 0)))
    return (current + spilled).reshape(row_count, -1).astype(jnp.bfloat16)


def dft_table(point_count, bin_count):
    sample_index = jnp.arange(point_count, dtype=jnp.int32)[:, None]
    frequency = 1 + jnp.arange(bin_count, dtype=jnp.int32)[None, :]
    angle = (sample_index * frequency % point_count).astype(jnp.float32) * (
        2.0 * math.pi / point_count
    )
    return jnp.concatenate([jnp.cos(angle), -jnp.sin(angle)], axis=1).astype(jnp.bfloat16)


def lag_table(point_count, bin_count, lag_count, window_count):
    frequency = 1 + jnp.arange(bin_count, dtype=jnp.int32)[:, None]
    shifted = jnp.arange(lag_count, dtype=jnp.int32)[None, :] - lag_count // 2 + point_count
    angle = (frequency * shifted % point_count).astype(jnp.float32) * (2.0 * math.pi / point_count)
    weight = 1.0 / math.sqrt(window_count * bin_count)
    return jnp.concatenate([jnp.cos(angle) * weight, -jnp.sin(angle) * weight], axis=0)


def smoother(bin_count, span_width):
    bin_index = jnp.arange(bin_count, dtype=jnp.int32)
    nearby = (jnp.abs(bin_index[:, None] - bin_index[None, :]) <= (span_width - 1) // 2).astype(
        jnp.float32
    )
    return nearby / jnp.sum(nearby, axis=0, keepdims=True)


def whiten(decimated):
    spectrum = jnp.dot(
        decimated, dft_table(decimated.shape[1], NBINS), preferred_element_type=jnp.float32
    )
    real_part = spectrum[:, :NBINS]
    imag_part = spectrum[:, NBINS:]
    magnitude = jnp.sqrt(real_part * real_part + imag_part * imag_part)
    smooth = jnp.dot(magnitude, smoother(NBINS, SMOOTH), precision=lax.Precision.HIGHEST)
    floor_level = water_level * jnp.mean(smooth, axis=1, keepdims=True) + epsilon
    factor = 1.0 / (smooth + floor_level)
    return (spectrum * jnp.concatenate([factor, factor], axis=1)).astype(jnp.bfloat16)


def block_start(block_index, chan_dev, wide_count, narrow_count):
    first_channel = block_index * BLK
    shard_index = first_channel // chan_dev
    return (
        shard_index % narrow_count * wide_count + shard_index // narrow_count
    ) * chan_dev + first_channel % chan_dev


def gather_rows(spectra, starts):

    def one_block(start_row):
        return lax.dynamic_slice_in_dim(spectra, start_row, BLK, 0)

    return jax.vmap(one_block)(starts)


def slot_cross(source, target, live_slots):
    highest = lax.Precision.HIGHEST
    src_real = source[..., :NBINS]
    src_imag = source[..., NBINS:]
    dst_real = target[..., :NBINS]
    dst_imag = target[..., NBINS:]
    real_sum = jnp.einsum("siwf,sjwf->ijsf", src_real, dst_real, precision=highest) + jnp.einsum(
        "siwf,sjwf->ijsf", src_imag, dst_imag, precision=highest
    )
    imag_sum = jnp.einsum("siwf,sjwf->ijsf", src_real, dst_imag, precision=highest) - jnp.einsum(
        "siwf,sjwf->ijsf", src_imag, dst_real, precision=highest
    )
    slot_count = source.shape[0]
    merged = jnp.concatenate(
        [
            real_sum.reshape(BLK * BLK, slot_count, NBINS),
            imag_sum.reshape(BLK * BLK, slot_count, NBINS),
        ],
        axis=2,
    )
    return merged * live_slots[None, :, None]


def stack_pairs(partial_value, window_count, wide_count):
    lag_basis = lag_table(NFFT, NBINS, LAGS, window_count)
    slot_count = partial_value.shape[1]
    pair_share = partial_value.shape[0] // wide_count
    summed = lax.psum_scatter(partial_value, "wide", scatter_dimension=0, tiled=True)
    flat = summed.reshape(pair_share * slot_count, 2 * NBINS)
    return jnp.dot(flat, lag_basis, precision=lax.Precision.HIGHEST).reshape(
        pair_share, slot_count, LAGS
    )


def on_device(raw_samples, filter_taps, tile_pairs, tile_owners):
    wide_count = lax.axis_size("wide")
    narrow_count = lax.axis_size("narrow")
    chan_dev = raw_samples.shape[0]
    window_total = raw_samples.shape[1]
    arrived = lax.all_to_all(raw_samples, "wide", split_axis=1, concat_axis=0, tiled=True)
    flat_rows = arrived.reshape(-1, arrived.shape[2])
    whitened = whiten(decimate(flat_rows, filter_taps)).reshape(
        arrived.shape[0], arrived.shape[1], 2 * NBINS
    )
    owner_index = lax.axis_index("narrow")
    slot_ids = jnp.arange(SLOTS, dtype=jnp.int32)
    owner_ids = jnp.arange(narrow_count, dtype=jnp.int32)
    owned_all = tile_owners[None, :] == owner_ids[:, None]
    rank_all = jnp.cumsum(owned_all.astype(jnp.int32), axis=1) - 1
    select_all = owned_all[:, None, :] & (rank_all[:, None, :] == slot_ids[None, :, None])
    select = lax.dynamic_index_in_dim(select_all, owner_index, 0, keepdims=False)
    pick_all = select_all.astype(jnp.int32)
    chosen_all = jnp.sum(pick_all[:, :, :, None] * tile_pairs[None, None, :, :], axis=2)
    chosen = lax.dynamic_index_in_dim(chosen_all, owner_index, 0, keepdims=False)
    live_slots = jnp.sum(select.astype(jnp.int32), axis=1).astype(jnp.float32)
    spectra = lax.all_gather(whitened, "narrow", axis=0, tiled=True)
    source = gather_rows(
        spectra, block_start(chosen[:, 0], chan_dev, wide_count, narrow_count)
    ).astype(jnp.float32)
    target = gather_rows(
        spectra, block_start(chosen[:, 1], chan_dev, wide_count, narrow_count)
    ).astype(jnp.float32)
    partial_value = slot_cross(source, target, live_slots)
    stacked = jnp.transpose(stack_pairs(partial_value, window_total, wide_count), (1, 0, 2))
    return stacked


def solution(mesh):
    in_specs = (P(("wide", "narrow"), None, None), P(), P(), P())
    out_specs = P("narrow", "wide", None)
    return jax.shard_map(
        on_device, mesh=mesh, in_specs=in_specs, out_specs=out_specs, check_vma=False
    )
```

profile of v0, /device:TPU:0, one launch (start us, length us, event | category | flops | bytes accessed | tf_op | source)
XLA Modules:
  0.0 474.6 jit_solution(13282219317979138211)
XLA Ops:
  6.5 11.2 %copy.33 = bf16[8,32,16384]{2,0,1:T(8,128)(2,1)} copy(bf16[8,32,16384]{2,1,0:T(8,128)(2,1)} %param.6) | data formatting | bytes 16777216 | tf_op args[0]
  17.7 7.7 %all-to-all-start = ((bf16[8,32,16384]{2,0,1:T(8,128)(2,1)}), bf16[8,32,16384]{2,0,1:T(8,128)(2,1)}, u32[]{:S(2)}, u32[]{:S(2)}) async-start(bf16[8,32,16384]{2,0,1:T(8,128)(2,1)} %copy.33), calls=%async_computation | async-start | bytes 16777216 | tf_op jit(solution)/shard_map/all_to_all | solution.py:141
  28.8 69.1 %cosine_convert_fusion = (bf16[4096,1024]{1,0:T(8,128)(2,1)}, bf16[4096,1024]{1,0:T(8,128)(2,1)}) fusion(s32[1024]{0:T(1024)S(1)} %iota_add_fusion), kind=kLoop, calls=%fused_computation.15 | loop fusion | flops 71303168 | bytes 16781312 | tf_op jit(solution)/shard_map/convert.24
  97.9 41.1 %all-to-all-done = bf16[8,32,16384]{2,0,1:T(8,128)(2,1)} async-done(((bf16[8,32,16384]{2,0,1:T(8,128)(2,1)}), bf16[8,32,16384]{2,0,1:T(8,128)(2,1)}, u32[]{:S(2)}, u32[]{:S(2)}) %all-to-all-start) | async-done | bytes 8388640 | tf_op jit(solution)/shard_map/all_to_all | solution.py:141
  138.9 13.5 %reshape_reshape.3 = bf16[8192,512]{1,0:T(8,128)(2,1)} reshape(bf16[32,8,1,16384]{3,1,0,2:T(8,128)(2,1)} %bitcast.65) | data formatting | bytes 16777216 | tf_op jit(solution)/shard_map/reshape;reshape | solution.py:37
  152.4 50.3 %convolution_bitcast_fusion = f32[8192,128]{0,1:T(8,128)} fusion(bf16[8192,512]{1,0:T(8,128)(2,1)} %reshape_reshape.3, bf16[]{:T(256)} %bitcast.63, bf16[]{:T(256)} %bitcast.62, bf16[]{:T(256)} %bitcast.61, bf16[]{:T(256)} %bitcast.60, bf16[]{:T(256)} %bitcast.59, bf16[]{:T(256)} %bitcast.58, bf16[]{:T(256)} %bitcast.57, bf16[]{:T(256)} %bitcast.56, ...), kind=kOutput, calls=%fused_computation.19 | convolution fusion | flops 1082916864 | bytes 12583552 | tf_op jit(solution)/shard_map/dot_general | solution.py:41
  202.7 45.8 %convolution_bitcast_fusion.1 = f32[8192,128]{0,1:T(8,128)} fusion(bf16[8192,512]{1,0:T(8,128)(2,1)S(1)} %bitcast.200, bf16[]{:T(256)} %bitcast.63, bf16[]{:T(256)} %bitcast.62, bf16[]{:T(256)} %bitcast.61, bf16[]{:T(256)} %bitcast.60, bf16[]{:T(256)} %bitcast.59, bf16[]{:T(256)} %bitcast.58, bf16[]{:T(256)} %bitcast.57, bf16[]{:T(256)} %bitcast.56, ...), kind=kOutput, calls=%fused_computation.20 | convolution fusion | flops 1082851328 | bytes 12583552 | tf_op jit(solution)/shard_map/dot_general | solution.py:38
  248.5 5.6 %copy.35 = f32[8192,128]{1,0:T(8,128)} copy(f32[8192,128]{0,1:T(8,128)} %convolution_bitcast_fusion) | data formatting | bytes 8388608 | tf_op jit(solution)/shard_map/dot_general | solution.py:41
  254.1 5.6 %copy.34 = f32[8192,128]{1,0:T(8,128)} copy(f32[8192,128]{0,1:T(8,128)} %convolution_bitcast_fusion.1) | data formatting | bytes 8388608 | tf_op jit(solution)/shard_map/dot_general | solution.py:38
  259.7 4.2 add_convert_fusion
  263.9 2.8 copy.36
  266.7 10.9 %fusion.3 = f32[256,2048]{1,0:T(8,128)S(1)} fusion(bf16[256,4096]{0,1:T(8,128)(2,1)} %bitcast.203, bf16[4096,1024]{1,0:T(8,128)(2,1)} %get-tuple-element.55, bf16[4096,1024]{1,0:T(8,128)(2,1)} %get-tuple-element.54), kind=kOutput, calls=%fused_computation.10 | convolution fusion | flops 4328521728 | bytes 20971520 | tf_op jit(solution)/shard_map/dot_general | solution.py:74
  277.6 3.8 fusion.583
  283.7 57.0 %all-gather.3.cloned.1.call-done = bf16[1024,2048]{1,0:T(8,128)(2,1)} async-done(((bf16[256,2048]{1,0:T(8,128)(2,1)}), bf16[1024,2048]{1,0:T(8,128)(2,1)}) %all-gather.3.cloned.1.call-update) | async-done | bytes 4194320 | tf_op jit(solution)/shard_map/all_gather | solution.py:157
  340.7 18.2 %while.2 = (s32[]{:T(128)}, bf16[1024,1,2048]{2,0,1:T(8,128)(2,1)}, s32[8,3]{0,1:T(4,128)S(1)}, bf16[8,8,1,2048]{3,1,2,0:T(8,128)(2,1)S(1)}, s32[]{:T(128)}) while((s32[]{:T(128)}, bf16[1024,1,2048]{2,0,1:T(8,128)(2,1)}, s32[8,3]{0,1:T(4,128)S(1)}, bf16[8,8,1,2048]{3,1,2,0:T(8,128)(2,1)S(1)}, s32[]{:T(128)}) %tuple.109), condition=%wide.while_cond, body=%wide.while_body.sunk | while | flops 2 | bytes 65641 | solution.py:97
  341.6 1.5 bitcast_dynamic-update-slice_fusion.4
  343.9 1.5 bitcast_dynamic-update-slice_fusion.4
  346.1 1.5 bitcast_dynamic-update-slice_fusion.4
  348.4 1.5 bitcast_dynamic-update-slice_fusion.4
  350.6 1.5 bitcast_dynamic-update-slice_fusion.4
  352.8 1.5 bitcast_dynamic-update-slice_fusion.4
  355.1 1.5 bitcast_dynamic-update-slice_fusion.4
  357.3 1.5 bitcast_dynamic-update-slice_fusion.4
  359.3 17.9 %while.3 = (s32[]{:T(128)}, bf16[1024,1,2048]{2,0,1:T(8,128)(2,1)}, s32[8,3]{0,1:T(4,128)S(1)}, bf16[8,8,1,2048]{3,1,2,0:T(8,128)(2,1)S(1)}, s32[]{:T(128)}) while((s32[]{:T(128)}, bf16[1024,1,2048]{2,0,1:T(8,128)(2,1)}, s32[8,3]{0,1:T(4,128)S(1)}, bf16[8,8,1,2048]{3,1,2,0:T(8,128)(2,1)S(1)}, s32[]{:T(128)}) %tuple.110), condition=%wide.while_cond.1, body=%wide.while_body.1.sunk | while | flops 2 | bytes 65641 | solution.py:97
  360.0 1.5 bitcast_dynamic-update-slice_fusion.5
  362.2 1.5 bitcast_dynamic-update-slice_fusion.5
  364.4 1.5 bitcast_dynamic-update-slice_fusion.5
  366.7 1.5 bitcast_dynamic-update-slice_fusion.5
  378.1 2.6 maximum_multiply_fusion
  380.8 9.7 %cosine_multiply_fusion = (f32[1024,512]{1,0:T(8,128)S(1)}, f32[1024,512]{1,0:T(8,128)}) fusion(s32[512]{0:T(512)S(1)} %iota_add_fusion.1, s32[1024]{0:T(1024)S(1)} %iota_add_fusion), kind=kLoop, calls=%fused_computation.42 | loop fusion | flops 8912896 | bytes 4200448 | tf_op jit(solution)/shard_map/mul | solution.py:62
  390.5 72.8 %reduce-scatter.2.cloned.1.call-done = f32[2,8,2048]{2,1,0:T(8,128)} async-done(((f32[64,8,2048]{2,1,0:T(8,128)}), f32[2,8,2048]{2,1,0:T(8,128)}) %reduce-scatter.2.cloned.1.call-update) | async-done | bytes 131088 | tf_op jit(solution)/shard_map/reduce_scatter | solution.py:129
  463.3 3.8 fusion.20
  (83 shorter events, 24.4 us)
Async XLA Ops:
  17.7 8.1 %copy-start = (f32[64]{0:T(128)S(1)}, f32[64]{0:T(128)}, u32[]{:S(2)}) copy-start(f32[64]{0:T(128)} %param.7) | copy-start | bytes 772
  17.7 121.2 %all-to-all-start = ((bf16[8,32,16384]{2,0,1:T(8,128)(2,1)}), bf16[8,32,16384]{2,0,1:T(8,128)(2,1)}, u32[]{:S(2)}, u32[]{:S(2)}) async-start(bf16[8,32,16384]{2,0,1:T(8,128)(2,1)} %copy.33), calls=%async_computation | async-start | bytes 16777216 | tf_op jit(solution)/shard_map/all_to_all | solution.py:141
  25.4 315.2 %all-gather.3.cloned.1.call-start = ((), (), s32[]{:S(2)}) async-start(), calls=%async_computation.3 | async-start | bytes 5242880 | tf_op jit(solution)/shard_map/all_gather | solution.py:157
  152.4 50.3 %slice-start = ((s8[8388608]{0:T(1024)(128)(4,1)}), s8[4194304]{0:T(1024)(128)(4,1)S(1)}, s32[]{:S(2)}) async-start(s8[8388608]{0:T(1024)(128)(4,1)} %bitcast.199), calls=%async_computation.4 | async-start | bytes 8388608
  152.4 50.3 %slice-start.1 = ((s8[8388608]{0:T(1024)(128)(4,1)}), s8[4194304]{0:T(1024)(128)(4,1)S(1)}, s32[]{:S(2)}) async-start(s8[8388608]{0:T(1024)(128)(4,1)} %bitcast.199), calls=%async_computation.5 | async-start | bytes 8388608
  281.4 1.6 copy-start.2
  281.4 1.8 copy-start.1
  283.0 180.3 %reduce-scatter.2.cloned.1.call-start = ((), (), s32[]{:S(2)}) async-start(), calls=%async_computation.2 | async-start | bytes 4325376 | tf_op jit(solution)/shard_map/reduce_scatter | solution.py:129
Sparse Core Ops, SparseCore 0:
  283.1 57.5 all-gather.2
  380.9 82.3 reduce-scatter.1
where the time goes:
time: 477 us; the launch traced here: 475 us
  waiting for transfers between devices  171 us (36%)
  matrix products  115 us (24%)
  other arithmetic  88.6 us (19%)
  local copies, waits for them, and re-layouts  78.4 us (16%)
  between operations  13.6 us (3%)
  starting transfers between devices  7.96 us (2%)
    reduce_scatter x1, waiting for transfers between devices, stack_pairs(): lax.psum_scatter(partial_value, 'wide', scatter_dimension=0, tiled=True)  72.8 us
    another operation x3, other arithmetic  69.2 us
    all_gather x1, waiting for transfers between devices, on_device(): spectra = lax.all_gather(whitened, 'narrow', axis=0, tiled=True)  57 us
    dot_general x1, matrix products, decimate(): jnp.dot(segments, last_table, preferred_element_type=jnp.float32)  50.3 us
    dot_general x1, matrix products, decimate(): jnp.dot(segments, this_table, preferred_element_type=jnp.float32)  45.8 us
    all_to_all x1, waiting for transfers between devices, on_device(): lax.all_to_all(raw_samples, 'wide', split_axis=1, concat_axis=0, tiled=True)  41.1 us
    gather x48, local copies, waits for them, and re-layouts  35.5 us
    another operation x1, local copies, waits for them, and re-layouts, decimate(): segments = samples.reshape(-1, DECIM * block_size)  13.5 us
  transfers between devices with their start and end apart: 3, of which 3 were waited for; matrix products, arithmetic and copies ran while one was open for 17% of the time, Pallas kernels for 0%

commit v1 on v0

--- a/solution.py
+++ b/solution.py
@@ -138,7 +138,14 @@
     narrow_count = lax.axis_size("narrow")
     chan_dev = raw_samples.shape[0]
     window_total = raw_samples.shape[1]
-    arrived = lax.all_to_all(raw_samples, "wide", split_axis=1, concat_axis=0, tiled=True)
+
+    def fill_core_over_axis(chunk, shard_axis):
+        outer = jax.lax.axis_size(shard_axis)
+        block_next = jnp.split(chunk, outer, axis=1)
+        new = jnp.stack(block_next, axis=0)
+        return jnp.concatenate(jax.lax.all_to_all(new, shard_axis, 0, 0), axis=0)
+
+    arrived = fill_core_over_axis(raw_samples, "wide")
     flat_rows = arrived.reshape(-1, arrived.shape[2])
     whitened = whiten(decimate(flat_rows, filter_taps)).reshape(
         arrived.shape[0], arrived.shape[1], 2 * NBINS

time: 477 us -> 513 us (1.075)
  local copies, waits for them, and re-layouts: 78.4 us -> 106 us
  matrix products: 115 us -> 124 us
    slice x0 -> x1, matrix products: none -> 55.8 us  [decimate(): spilled = jnp.pad(spilled[:, :-1], ((0, 0), (1, 0), (0, 0)))]
    dot_general x1 -> x0, matrix products: 50.3 us -> none  [decimate(): jnp.dot(segments, last_table, preferred_element_type=jnp.float32)]
    unnamed x13 -> x50, local copies, waits for them, and re-layouts: 11.3 us -> 41.5 us
    split x0 -> x2, local copies, waits for them, and re-layouts: none -> 25.3 us  [fill_core_over_axis(): block_next = jnp.split(chunk, outer, axis=1)]
    another operation x5, local copies, waits for them, and re-layouts: 14.1 us -> 1.63 us  [the longest x1 1 us: fill_core_over_axis(): new = jnp.stack(block_next, axis=0)]
    dot_general x2 -> x0, local copies, waits for them, and re-layouts: 11.2 us -> none  [the longest x1 5.61 us: decimate(): jnp.dot(segments, this_table, preferred_element_type=jnp.float32)]
  transfers between devices with their start and end apart: 3 -> 3, of which waited for: 3 -> 3; matrix products, arithmetic and copies ran while one was open for 17% -> 16% of each run, Pallas kernels for 0% -> 0%
where the time goes in v1:
time: 513 us; the launch traced here: 507 us
  waiting for transfers between devices  171 us (33%)
  matrix products  124 us (24%)
  local copies, waits for them, and re-layouts  106 us (21%)
  other arithmetic  84.6 us (16%)
  between operations  13.9 us (3%)
  starting transfers between devices  7.78 us (2%)
    reduce_scatter x1, waiting for transfers between devices, stack_pairs(): lax.psum_scatter(partial_value, 'wide', scatter_dimension=0, tiled=True)  72.8 us
    another operation x3, other arithmetic  69.4 us
    all_gather x1, waiting for transfers between devices, on_device(): spectra = lax.all_gather(whitened, 'narrow', axis=0, tiled=True)  57 us
    slice x1, matrix products, decimate(): spilled = jnp.pad(spilled[:, :-1], ((0, 0), (1, 0), (0, 0)))  55.8 us
    dot_general x1, matrix products, decimate(): jnp.dot(segments, this_table, preferred_element_type=jnp.float32)  48 us
    unnamed x50, local copies, waits for them, and re-layouts  41.5 us
    all_to_all x1, waiting for transfers between devices, fill_core_over_axis(): return jnp.concatenate(jax.lax.all_to_all(new, shard_axis, 0, 0), axis=0)  41.1 us
    gather x48, local copies, waits for them, and re-layouts  33.8 us
  transfers between devices with their start and end apart: 3, of which 3 were waited for; matrix products, arithmetic and copies ran while one was open for 16% of the time, Pallas kernels for 0%

profile of v1, /device:TPU:0, one launch (start us, length us, event | category | flops | bytes accessed | tf_op | source)
XLA Modules:
  0.0 507.4 jit_solution(3149457112491657716)
XLA Ops:
  6.5 14.1 %fusion.620 = (bf16[8,1,16384]{2,1,0:T(2,128)(2,1)S(1)}, bf16[8,1,16384]{2,1,0:T(2,128)(2,1)S(1)}, bf16[8,1,16384]{2,1,0:T(2,128)(2,1)S(1)}, bf16[8,1,16384]{2,1...) fusion(bf16[8,32,16384]{2,1,0:T(8,128)(2,1)} %param.6), kind=kLoop, calls=%fused_computation.716 | loop fusion | bytes 6815744 | tf_op jit(solution)/shard_map/split | solution.py:144
  20.7 11.2 %fusion.619 = (bf16[8,1,16384]{2,1,0:T(2,128)(2,1)S(1)}, bf16[8,1,16384]{2,1,0:T(2,128)(2,1)S(1)}, bf16[8,1,16384]{2,1,0:T(2,128)(2,1)S(1)}, bf16[8,1,16384]{2,1...) fusion(bf16[8,32,16384]{2,1,0:T(8,128)(2,1)S(1)} %copy-done), kind=kLoop, calls=%fused_computation.715 | loop fusion | bytes 9961472 | tf_op jit(solution)/shard_map/split | solution.py:144
  63.9 7.7 %all-to-all-start = ((bf16[32,8,1,16384]{3,1,2,0:T(8,128)(2,1)}), bf16[32,8,1,16384]{3,1,2,0:T(8,128)(2,1)}, u32[]{:S(2)}, u32[]{:S(2)}) async-start(bf16[32,8,1,16384]{3,1,2,0:T(8,128)(2,1)} %fusion.30), calls=%async_computation | async-start | bytes 16777216 | tf_op jit(solution)/shard_map/all_to_all | solution.py:146
  74.7 69.3 %cosine_convert_fusion = (bf16[4096,1024]{1,0:T(8,128)(2,1)}, bf16[4096,1024]{1,0:T(8,128)(2,1)}) fusion(s32[1024]{0:T(1024)S(1)} %iota_add_fusion), kind=kLoop, calls=%fused_computation.15 | loop fusion | flops 71303168 | bytes 16781312 | tf_op jit(solution)/shard_map/convert.24
  144.0 41.1 %all-to-all-done = bf16[32,8,1,16384]{3,1,2,0:T(8,128)(2,1)} async-done(((bf16[32,8,1,16384]{3,1,2,0:T(8,128)(2,1)}), bf16[32,8,1,16384]{3,1,2,0:T(8,128)(2,1)}, u32[]{:S(2)}, u32[]{:S(2)}) %all-to-all-start) | async-done | bytes 8388640 | tf_op jit(solution)/shard_map/all_to_all | solution.py:146
  185.1 10.4 %copy.155 = bf16[32,8,32,512]{3,2,1,0:T(8,128)(2,1)} copy(bf16[32,8,32,512]{3,1,2,0:T(8,128)(2,1)} %bitcast.192) | data formatting | bytes 16777216
  195.5 55.8 %fusion.10 = f32[256,31,128]{0,2,1:T(8,128)S(1)} fusion(bf16[256,32,512]{2,1,0:T(8,128)(2,1)} %bitcast.322, bf16[]{:T(256)} %bitcast.95, bf16[]{:T(256)} %bitcast.94, bf16[]{:T(256)} %bitcast.93, bf16[]{:T(256)} %bitcast.92, bf16[]{:T(256)} %bitcast.91, bf16[]{:T(256)} %bitcast.90, bf16[]{:T(256)} %bitcast.89, bf16[]{:T(256)} %bitcast.88, bf16[]{:T(256)} %bitcast.87, ...), kind=kOutput, calls=%fused_computation.19 | convolution fusion | flops 1049362432 | bytes 12452480 | tf_op jit(solution)/shard_map/slice | solution.py:44
  251.4 48.0 %add_convert_fusion = bf16[256,32,128]{0,2,1:T(8,128)(2,1)} fusion(f32[256,31,128]{0,2,1:T(8,128)S(1)} %fusion.10, bf16[256,32,512]{2,1,0:T(8,128)(2,1)S(1)} %bitcast.323, bf16[]{:T(256)} %bitcast.95, bf16[]{:T(256)} %bitcast.94, bf16[]{:T(256)} %bitcast.93, bf16[]{:T(256)} %bitcast.92, bf16[]{:T(256)} %bitcast.91, bf16[]{:T(256)} %bitcast.90, ...), kind=kOutput, calls=%fused_computation.31 | convolution fusion | flops 1084948480 | bytes 14549632 | tf_op jit(solution)/shard_map/dot_general | solution.py:38
  299.4 10.9 %fusion.3 = f32[256,2048]{1,0:T(8,128)} fusion(bf16[256,4096]{0,1:T(8,128)(2,1)} %bitcast.327, bf16[4096,1024]{1,0:T(8,128)(2,1)} %get-tuple-element.87, bf16[4096,1024]{1,0:T(8,128)(2,1)S(1)} %bitcast.321), kind=kOutput, calls=%fused_computation.10 | convolution fusion | flops 4328521728 | bytes 20971520 | tf_op jit(solution)/shard_map/dot_general | solution.py:74
  310.3 5.5 %fusion.625 = (f32[256]{0:T(256)S(1)}, f32[256,1024]{1,0:T(8,128)S(1)}) fusion(f32[1024]{0:T(1024)S(1)} %convert_reduce_fusion, f32[256,2048]{1,0:T(8,128)} %fusion.3), kind=kOutput, calls=%fused_computation.721 | convolution fusion | flops 3227516672 | bytes 3150848 | tf_op jit(solution)/shard_map/dot_general | solution.py:80
  318.1 57.0 %all-gather.3.cloned.1.call-done = bf16[1024,2048]{1,0:T(8,128)(2,1)} async-done(((bf16[256,2048]{1,0:T(8,128)(2,1)}), bf16[1024,2048]{1,0:T(8,128)(2,1)}) %all-gather.3.cloned.1.call-update) | async-done | bytes 4194320 | tf_op jit(solution)/shard_map/all_gather | solution.py:164
  375.0 17.2 %while.2 = (s32[]{:T(128)}, bf16[1024,1,2048]{2,0,1:T(8,128)(2,1)}, s32[8,3]{0,1:T(4,128)S(1)}, bf16[8,8,1,2048]{3,1,2,0:T(8,128)(2,1)S(1)}, s32[]{:T(128)}) while((s32[]{:T(128)}, bf16[1024,1,2048]{2,0,1:T(8,128)(2,1)}, s32[8,3]{0,1:T(4,128)S(1)}, bf16[8,8,1,2048]{3,1,2,0:T(8,128)(2,1)S(1)}, s32[]{:T(128)}) %tuple.139), condition=%wide.while_cond, body=%wide.while_body.sunk | while | flops 2 | bytes 65641 | solution.py:97
  375.9 1.5 bitcast_dynamic-update-slice_fusion.4
  378.0 1.5 bitcast_dynamic-update-slice_fusion.4
  380.2 1.5 bitcast_dynamic-update-slice_fusion.4
  382.3 1.5 bitcast_dynamic-update-slice_fusion.4
  384.4 1.5 bitcast_dynamic-update-slice_fusion.4
  386.5 1.5 bitcast_dynamic-update-slice_fusion.4
  388.7 1.5 bitcast_dynamic-update-slice_fusion.4
  390.8 1.5 bitcast_dynamic-update-slice_fusion.4
  392.7 17.0 %while.3 = (s32[]{:T(128)}, bf16[1024,1,2048]{2,0,1:T(8,128)(2,1)}, s32[8,3]{0,1:T(4,128)S(1)}, bf16[8,8,1,2048]{3,1,2,0:T(8,128)(2,1)S(1)}, s32[]{:T(128)}) while((s32[]{:T(128)}, bf16[1024,1,2048]{2,0,1:T(8,128)(2,1)}, s32[8,3]{0,1:T(4,128)S(1)}, bf16[8,8,1,2048]{3,1,2,0:T(8,128)(2,1)S(1)}, s32[]{:T(128)}) %tuple.140), condition=%wide.while_cond.1, body=%wide.while_body.1.sunk | while | flops 2 | bytes 65641 | solution.py:97
  393.3 1.5 bitcast_dynamic-update-slice_fusion.5
  395.5 1.5 bitcast_dynamic-update-slice_fusion.5
  397.6 1.5 bitcast_dynamic-update-slice_fusion.5
  399.7 1.5 bitcast_dynamic-update-slice_fusion.5
  401.9 1.5 bitcast_dynamic-update-slice_fusion.5
  404.0 1.5 bitcast_dynamic-update-slice_fusion.5
  408.2 1.5 bitcast_dynamic-update-slice_fusion.5
  410.7 2.6 maximum_multiply_fusion
  413.4 9.7 %cosine_multiply_fusion = (f32[1024,512]{1,0:T(8,128)S(1)}, f32[1024,512]{1,0:T(8,128)}) fusion(s32[512]{0:T(512)S(1)} %iota_add_fusion.1, s32[1024]{0:T(1024)S(1)} %iota_add_fusion), kind=kLoop, calls=%fused_computation.44 | loop fusion | flops 8912896 | bytes 4200448 | tf_op jit(solution)/shard_map/mul | solution.py:62
  423.1 72.8 %reduce-scatter.2.cloned.1.call-done = f32[2,8,2048]{2,1,0:T(8,128)} async-done(((f32[64,8,2048]{2,1,0:T(8,128)}), f32[2,8,2048]{2,1,0:T(8,128)}) %reduce-scatter.2.cloned.1.call-update) | async-done | bytes 131088 | tf_op jit(solution)/shard_map/reduce_scatter | solution.py:129
  495.9 3.8 fusion.26
  (118 shorter events, 50.7 us)
Async XLA Ops:
  6.5 14.1 %copy-start = (bf16[8,32,16384]{2,1,0:T(8,128)(2,1)S(1)}, bf16[8,32,16384]{2,1,0:T(8,128)(2,1)}, u32[]{:S(2)}) copy-start(bf16[8,32,16384]{2,1,0:T(8,128)(2,1)} %param.6) | copy-start | bytes 25165828
  63.9 8.0 %copy-start.2 = (f32[64]{0:T(128)S(1)}, f32[64]{0:T(128)}, u32[]{:S(2)}) copy-start(f32[64]{0:T(128)} %param.7) | copy-start | bytes 772
  63.9 121.2 %all-to-all-start = ((bf16[32,8,1,16384]{3,1,2,0:T(8,128)(2,1)}), bf16[32,8,1,16384]{3,1,2,0:T(8,128)(2,1)}, u32[]{:S(2)}, u32[]{:S(2)}) async-start(bf16[32,8,1,16384]{3,1,2,0:T(8,128)(2,1)} %fusion.30), calls=%async_computation | async-start | bytes 16777216 | tf_op jit(solution)/shard_map/all_to_all | solution.py:146
  71.6 303.4 %all-gather.3.cloned.1.call-start = ((), (), s32[]{:S(2)}) async-start(), calls=%async_computation.3 | async-start | bytes 5242880 | tf_op jit(solution)/shard_map/all_gather | solution.py:164
  195.5 55.8 %copy-start.1 = (bf16[32,8,32,512]{3,2,1,0:T(8,128)(2,1)S(1)}, bf16[32,8,32,512]{3,2,1,0:T(8,128)(2,1)}, u32[]{:S(2)}) copy-start(bf16[32,8,32,512]{3,2,1,0:T(8,128)(2,1)} %copy.155) | copy-start | bytes 25165828
  195.5 103.9 %slice-start = ((s8[8388608]{0:T(1024)(128)(4,1)}), s8[4194304]{0:T(1024)(128)(4,1)S(1)}, s32[]{:S(2)}) async-start(s8[8388608]{0:T(1024)(128)(4,1)} %bitcast.320), calls=%async_computation.4 | async-start | bytes 8388608
  251.4 48.1 %slice-start.1 = ((s8[8388608]{0:T(1024)(128)(4,1)}), s8[4194304]{0:T(1024)(128)(4,1)S(1)}, s32[]{:S(2)}) async-start(s8[8388608]{0:T(1024)(128)(4,1)} %bitcast.320), calls=%async_computation.5 | async-start | bytes 8388608
  310.3 5.8 %copy-start.3 = (f32[256,2048]{1,0:T(8,128)S(1)}, f32[256,2048]{1,0:T(8,128)}, u32[]{:S(2)}) copy-start(f32[256,2048]{1,0:T(8,128)} %fusion.3) | copy-start | bytes 6291460
  310.3 7.1 %copy-start.5 = (s32[16]{0:T(128)S(1)}, s32[16]{0:T(128)}, u32[]{:S(2)}) copy-start(s32[16]{0:T(128)} %param.9) | copy-start | bytes 196
  310.3 7.4 %copy-start.4 = (s32[16,2]{0,1:T(2,128)S(1)}, s32[16,2]{0,1:T(2,128)}, u32[]{:S(2)}) copy-start(s32[16,2]{0,1:T(2,128)} %param.8) | copy-start | bytes 388
  317.4 178.6 %reduce-scatter.2.cloned.1.call-start = ((), (), s32[]{:S(2)}) async-start(), calls=%async_computation.2 | async-start | bytes 4325376 | tf_op jit(solution)/shard_map/reduce_scatter | solution.py:129
Sparse Core Ops, SparseCore 0:
  317.5 57.5 all-gather.2
  413.5 82.3 reduce-scatter.1
